TPU v7x, 32 devices: a whole 2x2x4 slice. The times are simulated.
32 devices in a mesh: slab: 2 (over y), genome: 4 (over x, core), group: 4 (over z).
Axes of the slice: x: 2, y: 2, z: 4, core: 2. Of those that a mesh axis runs over, the one named last changes fastest.
Arguments:
- genotypes: bfloat16 [640, 12288], P(None, ('slab', 'genome', 'group')), parts along dimension 1, may hold values from -6 to 6
Outputs:
- ld_score: float32 [12288], P(('slab', 'genome', 'group')), parts along dimension 0
There are 2 independent parts, one for each index of `slab`. A program takes and returns all parts, laid end to end along the dimension named above; each array names one. Nothing has to cross between parts.
All inputs are finite; a program needn't handle non-finite values.
Results may differ from a plain program's by a relative error of at most 0.0003.
Values may be sent and summed in bfloat16 or wider, within the bound.
No kernel may reach another device: no remote copies, remote signals or barrier semaphores. Data moves between devices by JAX's collectives and lax.ppermute only.
A program may use at most 64 MiB of HBM per device.

v0:
```python
import jax
import jax.numpy as jnp
from jax import lax
from jax.sharding import PartitionSpec as P


def passed_along(block, axis, distance):
    devices = range(lax.axis_size(axis))
    route = [(i - distance, i) for i in devices if i - distance in devices]
    return lax.ppermute(block, axis, route)


def per_device(genotypes):
    scaling = 1.0 / genotypes.shape[0]

    def squares(columns):
        band = (
            lax.dot_general(
                genotypes, columns, (((0,), (0,)), ((), ())), preferred_element_type=jnp.float32
            )
            * scaling
        )
        return jnp.sum(band * band, axis=1)

    gathered = lax.all_gather(genotypes, "group", axis=1, tiled=True)
    following = passed_along(gathered, "genome", -1)
    ld_score = squares(gathered) + squares(following)
    return ld_score


def solution(mesh):
    placed = (P(None, ("slab", "genome", "group")),)
    return jax.shard_map(
        per_device,
        mesh=mesh,
        in_specs=placed,
        out_specs=P(("slab", "genome", "group")),
        check_vma=False,
    )
```

profile of v0, /device:TPU:1, one launch (start us, length us, event | category | flops | bytes accessed | tf_op | source)
XLA Modules:
  0.0 89.7 jit_solution(2843091351955072725)
XLA Ops:
  6.5 0.0 all-gather.2.cloned.1.call-start
  6.5 0.0 copy-start
  6.5 0.7 all-gather.2.cloned.1.call-update
  7.3 47.5 %all-gather.2.cloned.1.call-done = bf16[640,1536]{1,0:T(8,128)(2,1)} async-done(((bf16[640,384]{1,0:T(8,128)(2,1)}), bf16[640,1536]{1,0:T(8,128)(2,1)}) %all-gather.2.cloned.1.call-update) | async-done | bytes 1966096 | tf_op jit(solution)/shard_map/all_gather | solution.py:25
  54.7 2.7 %collective-permute-start = (bf16[640,1536]{1,0:T(8,128)(2,1)}, bf16[640,1536]{1,0:T(8,128)(2,1)S(1)}, u32[]{:S(2)}, u32[]{:S(2)}) collective-permute-start(bf16[640,1536]{1,0:T(8,128)(2,1)} %all-gather.2.cloned.1.call-done), channel_id=1, source_target_pairs={{4,0},{8,4},{12,8},{5,1},{9,5},{13,9},{6,2},{10,6},{14,10},{7,3},{... | collective-permute-start | bytes 5898248 | tf_op jit(solution)/shard_map/ppermute | solution.py:10
  57.5 2.9 %fusion.2 = f32[384]{0:T(512)S(1)} fusion(bf16[640,384]{1,0:T(8,128)(2,1)} %param.1, bf16[640,1536]{1,0:T(8,128)(2,1)} %all-gather.2.cloned.1.call-done), kind=kOutput, calls=%fused_computation.4 | convolution fusion | flops 756743808 | bytes 2459136 | tf_op jit(solution)/shard_map/dot_general | solution.py:18
  60.4 20.7 %collective-permute-done = bf16[640,1536]{1,0:T(8,128)(2,1)S(1)} collective-permute-done((bf16[640,1536]{1,0:T(8,128)(2,1)}, bf16[640,1536]{1,0:T(8,128)(2,1)S(1)}, u32[]{:S(2)}, u32[]{:S(2)}) %collective-permute-start) | collective-permute-done | bytes 1966112 | tf_op jit(solution)/shard_map/ppermute | solution.py:10
  81.1 0.0 copy-done
  81.1 1.2 %fusion.3 = f32[384]{0:T(512)S(1)} fusion(bf16[640,384]{1,0:T(8,128)(2,1)S(1)} %copy-done, bf16[640,1536]{1,0:T(8,128)(2,1)S(1)} %collective-permute-done), kind=kOutput, calls=%fused_computation.5 | convolution fusion | flops 756743808 | bytes 2459136 | tf_op jit(solution)/shard_map/dot_general | solution.py:18
  82.2 0.6 add.3
Async XLA Ops:
  6.5 48.2 %all-gather.2.cloned.1.call-start = ((), (), s32[]{:S(2)}) async-start(), calls=%async_computation | async-start | bytes 2457600 | tf_op jit(solution)/shard_map/all_gather | solution.py:25
  6.5 74.5 %copy-start = (bf16[640,384]{1,0:T(8,128)(2,1)S(1)}, bf16[640,384]{1,0:T(8,128)(2,1)}, u32[]{:S(2)}) copy-start(bf16[640,384]{1,0:T(8,128)(2,1)} %param.1) | copy-start | bytes 1474564
  54.7 26.3 %collective-permute-start = (bf16[640,1536]{1,0:T(8,128)(2,1)}, bf16[640,1536]{1,0:T(8,128)(2,1)S(1)}, u32[]{:S(2)}, u32[]{:S(2)}) collective-permute-start(bf16[640,1536]{1,0:T(8,128)(2,1)} %all-gather.2.cloned.1.call-done), channel_id=1, source_target_pairs={{4,0},{8,4},{12,8},{5,1},{9,5},{13,9},{6,2},{10,6},{14,10},{7,3},{... | collective-permute-start | bytes 5898248 | tf_op jit(solution)/shard_map/ppermute | solution.py:10
Sparse Core Ops, SparseCore 0:
  9.0 45.7 all-gather.1
where the time goes:
time: 89.8 us; the launch traced here: 89.7 us
  waiting for transfers between devices  68.8 us (77%)
  between operations  13.4 us (15%)
  matrix products  4.09 us (5%)
  starting transfers between devices  2.75 us (3%)
    all_gather x1, waiting for transfers between devices, per_device(): gathered = lax.all_gather(genotypes, 'group', axis=1, tiled=True)  47.5 us
    ppermute x1, waiting for transfers between devices, passed_along(): return lax.ppermute(block, axis, route)  20.7 us
    dot_general x2, matrix products, squares(): lax.dot_general(genotypes, columns, (((0,), (0,)), ((), ())), preferred_e...  4.09 us
    ppermute x1, starting transfers between devices, passed_along(): return lax.ppermute(block, axis, route)  2.75 us
  transfers between devices with their start and end apart: 2, of which 2 were waited for; matrix products, arithmetic and copies ran while one was open for 3% of the time, Pallas kernels for 0%

commit v1 on v0

--- a/solution.py
+++ b/solution.py
@@ -22,7 +22,16 @@
         )
         return jnp.sum(band * band, axis=1)
 
-    gathered = lax.all_gather(genotypes, "group", axis=1, tiled=True)
+    ways = lax.axis_size("group")
+    up = [(d, (d + 1) % ways) for d in range(ways)]
+    down = [(d, (d - 1) % ways) for d in range(ways)]
+    earlier, later = ([genotypes], [genotypes])
+    for _ in range(ways // 2):
+        earlier.append(lax.ppermute(earlier[-1], "group", up))
+    for _ in range((ways - 1) // 2):
+        later.append(lax.ppermute(later[-1], "group", down))
+    line = jnp.concatenate([*earlier[::-1], *later[1:]], axis=1)
+    gathered = jnp.roll(line, (lax.axis_index("group") - ways // 2) * genotypes.shape[1], axis=1)
     following = passed_along(gathered, "genome", -1)
     ld_score = squares(gathered) + squares(following)
     return ld_score

time: 89.8 us -> 68.8 us (0.77)
  waiting for transfers between devices: 68.8 us -> 52.7 us
  between operations: 13.4 us -> 0.1 us
  starting transfers between devices: 2.75 us -> 9.44 us
  local copies, waits for them, and re-layouts: 0.01 us -> 3.06 us
  matrix products: 4.09 us -> 2.69 us
    all_gather x1 -> x0, waiting for transfers between devices: 47.5 us -> none  [per_device(): gathered = lax.all_gather(genotypes, 'group', axis=1, tiled=True)]
    ppermute x0 -> x3, waiting for transfers between devices: none -> 30.9 us  [the longest x2 23.4 us: per_device(): earlier.append(lax.ppermute(earlier[-1], 'group', up))]
    ppermute x0 -> x3, starting transfers between devices: none -> 5.39 us  [the longest x1 3.26 us: per_device(): later.append(lax.ppermute(later[-1], 'group', down))]
    unnamed x2 -> x9, local copies, waits for them, and re-layouts: 0.01 us -> 1.8 us
    dot_general x2, matrix products: 4.09 us -> 2.69 us  [squares(): lax.dot_general(genotypes, columns, (((0,), (0,)), ((), ())), preferred_e...]
    ppermute x1, starting transfers between devices: 2.75 us -> 4.05 us  [passed_along(): return lax.ppermute(block, axis, route)]
    ppermute x1, waiting for transfers between devices: 20.7 us -> 21.9 us  [passed_along(): return lax.ppermute(block, axis, route)]
    dynamic_slice x0 -> x1, local copies, waits for them, and re-layouts: none -> 1.14 us  [per_device(): jnp.roll(line, (lax.axis_index('group') - ways // 2) * genotypes.shape[1]...]
  transfers between devices with their start and end apart: 2 -> 4, of which waited for: 2 -> 4; matrix products, arithmetic and copies ran while one was open for 3% -> 4% of each run, Pallas kernels for 0% -> 0%
where the time goes in v1:
time: 68.8 us; the launch traced here: 68.6 us
  waiting for transfers between devices  52.7 us (77%)
  starting transfers between devices  9.44 us (14%)
  local copies, waits for them, and re-layouts  3.06 us (4%)
  matrix products  2.69 us (4%)
    ppermute x2, waiting for transfers between devices, per_device(): earlier.append(lax.ppermute(earlier[-1], 'group', up))  23.4 us
    ppermute x1, waiting for transfers between devices, passed_along(): return lax.ppermute(block, axis, route)  21.9 us
    ppermute x1, waiting for transfers between devices, per_device(): later.append(lax.ppermute(later[-1], 'group', down))  7.5 us
    ppermute x1, starting transfers between devices, passed_along(): return lax.ppermute(block, axis, route)  4.05 us
    ppermute x1, starting transfers between devices, per_device(): later.append(lax.ppermute(later[-1], 'group', down))  3.26 us
    dot_general x2, matrix products, squares(): lax.dot_general(genotypes, columns, (((0,), (0,)), ((), ())), preferred_e...  2.69 us
    ppermute x2, starting transfers between devices, per_device(): earlier.append(lax.ppermute(earlier[-1], 'group', up))  2.13 us
    unnamed x9, local copies, waits for them, and re-layouts  1.8 us
  transfers between devices with their start and end apart: 4, of which 4 were waited for; matrix products, arithmetic and copies ran while one was open for 4% of the time, Pallas kernels for 0%

profile of v1, /device:TPU:1, one launch (start us, length us, event | category | flops | bytes accessed | tf_op | source)
XLA Modules:
  0.0 68.6 jit_solution(15264377606346620041)
XLA Ops:
  0.0 0.0 copy-start
  0.0 2.1 %collective-permute-start = (bf16[640,384]{1,0:T(8,128)(2,1)}, bf16[640,384]{1,0:T(8,128)(2,1)S(1)}, u32[]{:S(2)}, u32[]{:S(2)}) collective-permute-start(bf16[640,384]{1,0:T(8,128)(2,1)} %param.1), channel_id=1, source_target_pairs={{0,1},{1,2},{2,3},{3,0},{4,5},{5,6},{6,7},{7,4},{8,9},{9,10},{10,1... | collective-permute-start | bytes 1474568 | tf_op jit(solution)/shard_map/ppermute | solution.py:30
  2.1 13.3 %collective-permute-done = bf16[640,384]{1,0:T(8,128)(2,1)S(1)} collective-permute-done((bf16[640,384]{1,0:T(8,128)(2,1)}, bf16[640,384]{1,0:T(8,128)(2,1)S(1)}, u32[]{:S(2)}, u32[]{:S(2)}) %collective-permute-start) | collective-permute-done | bytes 491552 | tf_op jit(solution)/shard_map/ppermute | solution.py:30
  15.4 0.0 collective-permute-start.1
  15.4 3.3 %collective-permute-start.2 = (bf16[640,384]{1,0:T(8,128)(2,1)}, bf16[640,384]{1,0:T(8,128)(2,1)S(1)}, u32[]{:S(2)}, u32[]{:S(2)}) collective-permute-start(bf16[640,384]{1,0:T(8,128)(2,1)} %param.1), channel_id=1, source_target_pairs={{0,3},{1,0},{2,1},{3,2},{4,7},{5,4},{6,5},{7,6},{8,11},{9,8},{10,9... | collective-permute-start | bytes 1474568 | tf_op jit(solution)/shard_map/ppermute | solution.py:32
  18.6 10.1 %collective-permute-done.1 = bf16[640,384]{1,0:T(8,128)(2,1)S(1)} collective-permute-done((bf16[640,384]{1,0:T(8,128)(2,1)S(1)}, bf16[640,384]{1,0:T(8,128)(2,1)S(1)}, u32[]{:S(2)}, u32[]{:S(2)}) %collective-permute-start.1) | collective-permute-done | bytes 491552 | tf_op jit(solution)/shard_map/ppermute | solution.py:30
  28.8 0.1 constant_dynamic-update-slice_fusion.7
  28.8 0.1 constant_dynamic-update-slice_fusion.6
  29.0 1.1 %constant_dynamic-update-slice_fusion.5 = bf16[640,3072]{1,0:T(8,128)(2,1)S(1)} fusion(bf16[640,3072]{1,0:T(8,128)(2,1)S(1)} %constant_dynamic-update-slice_fusion.6, bf16[640,384]{1,0:T(8,128)(2,1)} %param.1), kind=kLoop, calls=%fused_computation.11 | loop fusion | bytes 983040
  30.1 7.5 %collective-permute-done.2 = bf16[640,384]{1,0:T(8,128)(2,1)S(1)} collective-permute-done((bf16[640,384]{1,0:T(8,128)(2,1)}, bf16[640,384]{1,0:T(8,128)(2,1)S(1)}, u32[]{:S(2)}, u32[]{:S(2)}) %collective-permute-start.2) | collective-permute-done | bytes 491552 | tf_op jit(solution)/shard_map/ppermute | solution.py:32
  37.6 0.1 constant_dynamic-update-slice_fusion.4
  37.7 0.1 constant_dynamic-update-slice_fusion.3
  37.9 0.1 constant_dynamic-update-slice_fusion.2
  38.0 0.0 copy-done
  38.0 0.1 constant_dynamic-update-slice_fusion.1
  38.1 0.1 constant_dynamic-update-slice_fusion
  38.2 1.1 %constant_dynamic-slice_fusion = bf16[640,1536]{1,0:T(8,128)(2,1)S(1)} fusion(bf16[640,3072]{1,0:T(8,128)(2,1)S(1)} %constant_dynamic-update-slice_fusion, s32[]{:T(128)S(6)} %select_n.14), kind=kLoop, calls=%fused_computation.14 | loop fusion | bytes 3932164 | tf_op jit(solution)/shard_map/jit(_roll_dynamic)/dynamic_slice | solution.py:34
  39.4 4.0 %collective-permute-start.3 = (bf16[640,1536]{1,0:T(8,128)(2,1)S(1)}, bf16[640,1536]{1,0:T(8,128)(2,1)S(1)}, u32[]{:S(2)}, u32[]{:S(2)}) collective-permute-start(bf16[640,1536]{1,0:T(8,128)(2,1)S(1)} %constant_dynamic-slice_fusion), channel_id=1, source_target_pairs={{4,0},{8,4},{12,8},{5,1},{9,5},{13,9},{6,2},{10,6},{14,10},{7,3},{... | collective-permute-start | bytes 5898248 | tf_op jit(solution)/shard_map/ppermute | solution.py:10
  43.4 1.3 %fusion.2 = f32[384]{0:T(512)S(1)} fusion(bf16[640,1536]{1,0:T(8,128)(2,1)S(1)} %constant_dynamic-slice_fusion, bf16[640,384]{1,0:T(8,128)(2,1)S(1)} %copy-done), kind=kOutput, calls=%fused_computation.4 | convolution fusion | flops 756743808 | bytes 2459136 | tf_op jit(solution)/shard_map/dot_general | solution.py:18
  44.8 21.9 %collective-permute-done.3 = bf16[640,1536]{1,0:T(8,128)(2,1)S(1)} collective-permute-done((bf16[640,1536]{1,0:T(8,128)(2,1)S(1)}, bf16[640,1536]{1,0:T(8,128)(2,1)S(1)}, u32[]{:S(2)}, u32[]{:S(2)}) %collective-permute-start.3) | collective-permute-done | bytes 1966112 | tf_op jit(solution)/shard_map/ppermute | solution.py:10
  66.7 1.3 %fusion.3 = f32[384]{0:T(512)S(1)} fusion(bf16[640,1536]{1,0:T(8,128)(2,1)S(1)} %collective-permute-done.3, bf16[640,384]{1,0:T(8,128)(2,1)S(1)} %copy-done), kind=kOutput, calls=%fused_computation.5 | convolution fusion | flops 756743808 | bytes 2459136 | tf_op jit(solution)/shard_map/dot_general | solution.py:18
  68.0 0.6 add.16
Async XLA Ops:
  0.0 38.0 %copy-start = (bf16[640,384]{1,0:T(8,128)(2,1)S(1)}, bf16[640,384]{1,0:T(8,128)(2,1)}, u32[]{:S(2)}) copy-start(bf16[640,384]{1,0:T(8,128)(2,1)} %param.1) | copy-start | bytes 1474564
  0.0 15.4 %collective-permute-start = (bf16[640,384]{1,0:T(8,128)(2,1)}, bf16[640,384]{1,0:T(8,128)(2,1)S(1)}, u32[]{:S(2)}, u32[]{:S(2)}) collective-permute-start(bf16[640,384]{1,0:T(8,128)(2,1)} %param.1), channel_id=1, source_target_pairs={{0,1},{1,2},{2,3},{3,0},{4,5},{5,6},{6,7},{7,4},{8,9},{9,10},{10,1... | collective-permute-start | bytes 1474568 | tf_op jit(solution)/shard_map/ppermute | solution.py:30
  15.4 13.4 %collective-permute-start.1 = (bf16[640,384]{1,0:T(8,128)(2,1)S(1)}, bf16[640,384]{1,0:T(8,128)(2,1)S(1)}, u32[]{:S(2)}, u32[]{:S(2)}) collective-permute-start(bf16[640,384]{1,0:T(8,128)(2,1)S(1)} %collective-permute-done), channel_id=1, source_target_pairs={{0,1},{1,2},{2,3},{3,0},{4,5},{5,6},{6,7},{7,4},{8,9},{9,10},{10,1... | collective-permute-start | bytes 1474568 | tf_op jit(solution)/shard_map/ppermute | solution.py:30
  15.4 22.2 %collective-permute-start.2 = (bf16[640,384]{1,0:T(8,128)(2,1)}, bf16[640,384]{1,0:T(8,128)(2,1)S(1)}, u32[]{:S(2)}, u32[]{:S(2)}) collective-permute-start(bf16[640,384]{1,0:T(8,128)(2,1)} %param.1), channel_id=1, source_target_pairs={{0,3},{1,0},{2,1},{3,2},{4,7},{5,4},{6,5},{7,6},{8,11},{9,8},{10,9... | collective-permute-start | bytes 1474568 | tf_op jit(solution)/shard_map/ppermute | solution.py:32
  39.4 27.3 %collective-permute-start.3 = (bf16[640,1536]{1,0:T(8,128)(2,1)S(1)}, bf16[640,1536]{1,0:T(8,128)(2,1)S(1)}, u32[]{:S(2)}, u32[]{:S(2)}) collective-permute-start(bf16[640,1536]{1,0:T(8,128)(2,1)S(1)} %constant_dynamic-slice_fusion), channel_id=1, source_target_pairs={{4,0},{8,4},{12,8},{5,1},{9,5},{13,9},{6,2},{10,6},{14,10},{7,3},{... | collective-permute-start | bytes 5898248 | tf_op jit(solution)/shard_map/ppermute | solution.py:10
